TPU v7x, 32 devices: a whole 2x2x4 slice. The times are simulated.
32 devices in a mesh: slab: 2 (over y), genome: 4 (over x, core), group: 4 (over z).
Axes of the slice: x: 2, y: 2, z: 4, core: 2. Of those that a mesh axis runs over, the one named last changes fastest.
Arguments:
- genotypes: bfloat16 [640, 12288], P(None, ('slab', 'genome', 'group')), parts along dimension 1, may hold values from -6 to 6
Outputs:
- ld_score: float32 [12288], P(('slab', 'genome', 'group')), parts along dimension 0
There are 2 independent parts, one for each index of `slab`. A program takes and returns all parts, laid end to end along the dimension named above; each array names one. Nothing has to cross between parts.
All inputs are finite; a program needn't handle non-finite values.
Results may differ from a plain program's by a relative error of at most 0.0003.
Values may be sent and summed in bfloat16 or wider, within the bound.
No kernel may reach another device: no remote copies, remote signals or barrier semaphores. Data moves between devices by JAX's collectives and lax.ppermute only.
A program may use at most 64 MiB of HBM per device.

v0:
```python
import jax
import jax.numpy as jnp
from jax import lax
from jax.sharding import PartitionSpec as P


def passed_along(block, axis, distance):
    devices = range(lax.axis_size(axis))
    route = [(i - distance, i) for i in devices if i - distance in devices]
    return lax.ppermute(block, axis, route)


def per_device(genotypes):
    scaling = 1.0 / genotypes.shape[0]

    def squares(columns):
        band = (
            lax.dot_general(
                genotypes, columns, (((0,), (0,)), ((), ())), preferred_element_type=jnp.float32
            )
            * scaling
        )
        return jnp.sum(band * band, axis=1)

    gathered = lax.all_gather(genotypes, "group", axis=1, tiled=True)
    following = passed_along(gathered, "genome", -1)
    ld_score = squares(gathered) + squares(following)
    return ld_score


def solution(mesh):
    placed = (P(None, ("slab", "genome", "group")),)
    return jax.shard_map(
        per_device,
        mesh=mesh,
        in_specs=placed,
        out_specs=P(("slab", "genome", "group")),
        check_vma=False,
    )
```

profile of v0, /device:TPU:1, one launch (start us, length us, event | category | flops | bytes accessed | tf_op | source)
XLA Modules:
  0.0 89.7 jit_solution(2843091351955072725)
XLA Ops:
  6.5 0.0 all-gather.2.cloned.1.call-start
  6.5 0.0 copy-start
  6.5 0.7 all-gather.2.cloned.1.call-update
  7.3 47.5 %all-gather.2.cloned.1.call-done = bf16[640,1536]{1,0:T(8,128)(2,1)} async-done(((bf16[640,384]{1,0:T(8,128)(2,1)}), bf16[640,1536]{1,0:T(8,128)(2,1)}) %all-gather.2.cloned.1.call-update) | async-done | bytes 1966096 | tf_op jit(solution)/shard_map/all_gather | solution.py:25
  54.7 2.7 %collective-permute-start = (bf16[640,1536]{1,0:T(8,128)(2,1)}, bf16[640,1536]{1,0:T(8,128)(2,1)S(1)}, u32[]{:S(2)}, u32[]{:S(2)}) collective-permute-start(bf16[640,1536]{1,0:T(8,128)(2,1)} %all-gather.2.cloned.1.call-done), channel_id=1, source_target_pairs={{4,0},{8,4},{12,8},{5,1},{9,5},{13,9},{6,2},{10,6},{14,10},{7,3},{... | collective-permute-start | bytes 5898248 | tf_op jit(solution)/shard_map/ppermute | solution.py:10
  57.5 2.9 %fusion.2 = f32[384]{0:T(512)S(1)} fusion(bf16[640,384]{1,0:T(8,128)(2,1)} %param.1, bf16[640,1536]{1,0:T(8,128)(2,1)} %all-gather.2.cloned.1.call-done), kind=kOutput, calls=%fused_computation.4 | convolution fusion | flops 756743808 | bytes 2459136 | tf_op jit(solution)/shard_map/dot_general | solution.py:18
  60.4 20.7 %collective-permute-done = bf16[640,1536]{1,0:T(8,128)(2,1)S(1)} collective-permute-done((bf16[640,1536]{1,0:T(8,128)(2,1)}, bf16[640,1536]{1,0:T(8,128)(2,1)S(1)}, u32[]{:S(2)}, u32[]{:S(2)}) %collective-permute-start) | collective-permute-done | bytes 1966112 | tf_op jit(solution)/shard_map/ppermute | solution.py:10
  81.1 0.0 copy-done
  81.1 1.2 %fusion.3 = f32[384]{0:T(512)S(1)} fusion(bf16[640,384]{1,0:T(8,128)(2,1)S(1)} %copy-done, bf16[640,1536]{1,0:T(8,128)(2,1)S(1)} %collective-permute-done), kind=kOutput, calls=%fused_computation.5 | convolution fusion | flops 756743808 | bytes 2459136 | tf_op jit(solution)/shard_map/dot_general | solution.py:18
  82.2 0.6 add.3
Async XLA Ops:
  6.5 48.2 %all-gather.2.cloned.1.call-start = ((), (), s32[]{:S(2)}) async-start(), calls=%async_computation | async-start | bytes 2457600 | tf_op jit(solution)/shard_map/all_gather | solution.py:25
  6.5 74.5 %copy-start = (bf16[640,384]{1,0:T(8,128)(2,1)S(1)}, bf16[640,384]{1,0:T(8,128)(2,1)}, u32[]{:S(2)}) copy-start(bf16[640,384]{1,0:T(8,128)(2,1)} %param.1) | copy-start | bytes 1474564
  54.7 26.3 %collective-permute-start = (bf16[640,1536]{1,0:T(8,128)(2,1)}, bf16[640,1536]{1,0:T(8,128)(2,1)S(1)}, u32[]{:S(2)}, u32[]{:S(2)}) collective-permute-start(bf16[640,1536]{1,0:T(8,128)(2,1)} %all-gather.2.cloned.1.call-done), channel_id=1, source_target_pairs={{4,0},{8,4},{12,8},{5,1},{9,5},{13,9},{6,2},{10,6},{14,10},{7,3},{... | collective-permute-start | bytes 5898248 | tf_op jit(solution)/shard_map/ppermute | solution.py:10
Sparse Core Ops, SparseCore 0:
  9.0 45.7 all-gather.1
where the time goes:
time: 89.8 us; the launch traced here: 89.7 us
  waiting for transfers between devices  68.8 us (77%)
  between operations  13.4 us (15%)
  matrix products  4.09 us (5%)
  starting transfers between devices  2.75 us (3%)
    all_gather x1, waiting for transfers between devices, per_device(): gathered = lax.all_gather(genotypes, 'group', axis=1, tiled=True)  47.5 us
    ppermute x1, waiting for transfers between devices, passed_along(): return lax.ppermute(block, axis, route)  20.7 us
    dot_general x2, matrix products, squares(): lax.dot_general(genotypes, columns, (((0,), (0,)), ((), ())), preferred_e...  4.09 us
    ppermute x1, starting transfers between devices, passed_along(): return lax.ppermute(block, axis, route)  2.75 us
  transfers between devices with their start and end apart: 2, of which 2 were waited for; matrix products, arithmetic and copies ran while one was open for 3% of the time, Pallas kernels for 0%

commit v1 on v0

--- a/solution.py
+++ b/solution.py
@@ -2,6 +2,19 @@
 import jax.numpy as jnp
 from jax import lax
 from jax.sharding import PartitionSpec as P
+
+
+def perform_slices_here(z_in, chip_axis):
+    pile = [z_in]
+    axis_len = jax.lax.axis_size(chip_axis)
+    for t in [*range(axis_len - 1)]:
+        pile.append(
+            jax.lax.ppermute(
+                pile[-1], chip_axis, [(h, (h + 1) % axis_len) for h in range(axis_len)]
+            )
+        )
+    t1 = jnp.concatenate(pile[::-1], axis=1)
+    return jnp.roll(t1, (jax.lax.axis_index(chip_axis) + 1) * z_in.shape[1], axis=1)
 
 
 def passed_along(block, axis, distance):
@@ -22,7 +35,7 @@
         )
         return jnp.sum(band * band, axis=1)
 
-    gathered = lax.all_gather(genotypes, "group", axis=1, tiled=True)
+    gathered = perform_slices_here(genotypes, "group")
     following = passed_along(gathered, "genome", -1)
     ld_score = squares(gathered) + squares(following)
     return ld_score

time: 89.8 us -> 74.3 us (0.83)
  between operations: 13.4 us -> 0.1 us
  waiting for transfers between devices: 68.8 us -> 60.6 us
  starting transfers between devices: 2.75 us -> 7.11 us
  local copies, waits for them, and re-layouts: 0.01 us -> 3.07 us
  matrix products: 4.09 us -> 2.69 us
    all_gather x1 -> x0, waiting for transfers between devices: 47.5 us -> none  [per_device(): gathered = lax.all_gather(genotypes, 'group', axis=1, tiled=True)]
    ppermute x0 -> x3, waiting for transfers between devices: none -> 38.9 us  [perform_slices_here(): jax.lax.ppermute(pile[-1], chip_axis, [(h, (h + 1) % axis_len) for h in r...]
    ppermute x1, starting transfers between devices: 2.75 us -> 4.98 us  [passed_along(): return lax.ppermute(block, axis, route)]
    ppermute x0 -> x3, starting transfers between devices: none -> 2.13 us  [perform_slices_here(): jax.lax.ppermute(pile[-1], chip_axis, [(h, (h + 1) % axis_len) for h in r...]
    unnamed x2 -> x9, local copies, waits for them, and re-layouts: 0.01 us -> 1.8 us
    dot_general x2, matrix products: 4.09 us -> 2.69 us  [squares(): lax.dot_general(genotypes, columns, (((0,), (0,)), ((), ())), preferred_e...]
    dynamic_slice x0 -> x1, local copies, waits for them, and re-layouts: none -> 1.15 us  [perform_slices_here(): jnp.roll(t1, (jax.lax.axis_index(chip_axis) + 1) * z_in.shape[1], axis=1)]
    ppermute x1, waiting for transfers between devices: 20.7 us -> 21.7 us  [passed_along(): return lax.ppermute(block, axis, route)]
  transfers between devices with their start and end apart: 2 -> 4, of which waited for: 2 -> 4; matrix products, arithmetic and copies ran while one was open for 3% -> 2% of each run, Pallas kernels for 0% -> 0%
where the time goes in v1:
time: 74.3 us; the launch traced here: 74.1 us
  waiting for transfers between devices  60.6 us (82%)
  starting transfers between devices  7.11 us (10%)
  local copies, waits for them, and re-layouts  3.07 us (4%)
  matrix products  2.69 us (4%)
    ppermute x3, waiting for transfers between devices, perform_slices_here(): jax.lax.ppermute(pile[-1], chip_axis, [(h, (h + 1) % axis_len) for h in r...  38.9 us
    ppermute x1, waiting for transfers between devices, passed_along(): return lax.ppermute(block, axis, route)  21.7 us
    ppermute x1, starting transfers between devices, passed_along(): return lax.ppermute(block, axis, route)  4.98 us
    dot_general x2, matrix products, squares(): lax.dot_general(genotypes, columns, (((0,), (0,)), ((), ())), preferred_e...  2.69 us
    ppermute x3, starting transfers between devices, perform_slices_here(): jax.lax.ppermute(pile[-1], chip_axis, [(h, (h + 1) % axis_len) for h in r...  2.13 us
    unnamed x9, local copies, waits for them, and re-layouts  1.8 us
  transfers between devices with their start and end apart: 4, of which 4 were waited for; matrix products, arithmetic and copies ran while one was open for 2% of the time, Pallas kernels for 0%

profile of v1, /device:TPU:1, one launch (start us, length us, event | category | flops | bytes accessed | tf_op | source)
XLA Modules:
  0.0 74.1 jit_solution(3866035682635391593)
XLA Ops:
  0.0 0.0 copy-start
  0.0 2.1 %collective-permute-start = (bf16[640,384]{1,0:T(8,128)(2,1)}, bf16[640,384]{1,0:T(8,128)(2,1)S(1)}, u32[]{:S(2)}, u32[]{:S(2)}) collective-permute-start(bf16[640,384]{1,0:T(8,128)(2,1)} %param.1), channel_id=1, source_target_pairs={{0,1},{1,2},{2,3},{3,0},{4,5},{5,6},{6,7},{7,4},{8,9},{9,10},{10,1... | collective-permute-start | bytes 1474568 | tf_op jit(solution)/shard_map/ppermute | solution.py:12
  2.1 13.3 %collective-permute-done = bf16[640,384]{1,0:T(8,128)(2,1)S(1)} collective-permute-done((bf16[640,384]{1,0:T(8,128)(2,1)}, bf16[640,384]{1,0:T(8,128)(2,1)S(1)}, u32[]{:S(2)}, u32[]{:S(2)}) %collective-permute-start) | collective-permute-done | bytes 491552 | tf_op jit(solution)/shard_map/ppermute | solution.py:12
  15.4 0.0 collective-permute-start.1
  15.4 13.3 %collective-permute-done.1 = bf16[640,384]{1,0:T(8,128)(2,1)S(1)} collective-permute-done((bf16[640,384]{1,0:T(8,128)(2,1)S(1)}, bf16[640,384]{1,0:T(8,128)(2,1)S(1)}, u32[]{:S(2)}, u32[]{:S(2)}) %collective-permute-start.1) | collective-permute-done | bytes 491552 | tf_op jit(solution)/shard_map/ppermute | solution.py:12
  28.7 0.0 collective-permute-start.2
  28.7 12.4 %collective-permute-done.2 = bf16[640,384]{1,0:T(8,128)(2,1)S(1)} collective-permute-done((bf16[640,384]{1,0:T(8,128)(2,1)S(1)}, bf16[640,384]{1,0:T(8,128)(2,1)S(1)}, u32[]{:S(2)}, u32[]{:S(2)}) %collective-permute-start.2) | collective-permute-done | bytes 491552 | tf_op jit(solution)/shard_map/ppermute | solution.py:12
  41.0 0.1 constant_dynamic-update-slice_fusion.7
  41.1 0.1 constant_dynamic-update-slice_fusion.6
  41.2 0.1 constant_dynamic-update-slice_fusion.5
  41.4 1.1 %constant_dynamic-update-slice_fusion.4 = bf16[640,3072]{1,0:T(8,128)(2,1)S(1)} fusion(bf16[640,3072]{1,0:T(8,128)(2,1)S(1)} %constant_dynamic-update-slice_fusion.5, bf16[640,384]{1,0:T(8,128)(2,1)} %param.1), kind=kLoop, calls=%fused_computation.10 | loop fusion | bytes 983040
  42.5 0.1 constant_dynamic-update-slice_fusion.3
  42.6 0.1 constant_dynamic-update-slice_fusion.2
  42.8 0.1 constant_dynamic-update-slice_fusion.1
  42.9 0.0 copy-done
  42.9 0.1 constant_dynamic-update-slice_fusion
  43.0 1.2 %constant_dynamic-slice_fusion = bf16[640,1536]{1,0:T(8,128)(2,1)S(1)} fusion(bf16[640,3072]{1,0:T(8,128)(2,1)S(1)} %constant_dynamic-update-slice_fusion, s32[]{:T(128)S(6)} %select_n.14), kind=kLoop, calls=%fused_computation.14 | loop fusion | bytes 3932164 | tf_op jit(solution)/shard_map/jit(_roll_dynamic)/dynamic_slice | solution.py:17
  44.2 5.0 %collective-permute-start.3 = (bf16[640,1536]{1,0:T(8,128)(2,1)S(1)}, bf16[640,1536]{1,0:T(8,128)(2,1)S(1)}, u32[]{:S(2)}, u32[]{:S(2)}) collective-permute-start(bf16[640,1536]{1,0:T(8,128)(2,1)S(1)} %constant_dynamic-slice_fusion), channel_id=1, source_target_pairs={{4,0},{8,4},{12,8},{5,1},{9,5},{13,9},{6,2},{10,6},{14,10},{7,3},{... | collective-permute-start | bytes 5898248 | tf_op jit(solution)/shard_map/ppermute | solution.py:23
  49.2 1.3 %fusion.2 = f32[384]{0:T(512)S(1)} fusion(bf16[640,1536]{1,0:T(8,128)(2,1)S(1)} %constant_dynamic-slice_fusion, bf16[640,384]{1,0:T(8,128)(2,1)S(1)} %copy-done), kind=kOutput, calls=%fused_computation.4 | convolution fusion | flops 756743808 | bytes 2459136 | tf_op jit(solution)/shard_map/dot_general | solution.py:31
  50.5 21.7 %collective-permute-done.3 = bf16[640,1536]{1,0:T(8,128)(2,1)S(1)} collective-permute-done((bf16[640,1536]{1,0:T(8,128)(2,1)S(1)}, bf16[640,1536]{1,0:T(8,128)(2,1)S(1)}, u32[]{:S(2)}, u32[]{:S(2)}) %collective-permute-start.3) | collective-permute-done | bytes 1966112 | tf_op jit(solution)/shard_map/ppermute | solution.py:23
  72.2 1.3 %fusion.3 = f32[384]{0:T(512)S(1)} fusion(bf16[640,1536]{1,0:T(8,128)(2,1)S(1)} %collective-permute-done.3, bf16[640,384]{1,0:T(8,128)(2,1)S(1)} %copy-done), kind=kOutput, calls=%fused_computation.5 | convolution fusion | flops 756743808 | bytes 2459136 | tf_op jit(solution)/shard_map/dot_general | solution.py:31
  73.6 0.6 add.19
Async XLA Ops:
  0.0 42.9 %copy-start = (bf16[640,384]{1,0:T(8,128)(2,1)S(1)}, bf16[640,384]{1,0:T(8,128)(2,1)}, u32[]{:S(2)}) copy-start(bf16[640,384]{1,0:T(8,128)(2,1)} %param.1) | copy-start | bytes 1474564
  0.0 15.4 %collective-permute-start = (bf16[640,384]{1,0:T(8,128)(2,1)}, bf16[640,384]{1,0:T(8,128)(2,1)S(1)}, u32[]{:S(2)}, u32[]{:S(2)}) collective-permute-start(bf16[640,384]{1,0:T(8,128)(2,1)} %param.1), channel_id=1, source_target_pairs={{0,1},{1,2},{2,3},{3,0},{4,5},{5,6},{6,7},{7,4},{8,9},{9,10},{10,1... | collective-permute-start | bytes 1474568 | tf_op jit(solution)/shard_map/ppermute | solution.py:12
  15.4 13.3 %collective-permute-start.1 = (bf16[640,384]{1,0:T(8,128)(2,1)S(1)}, bf16[640,384]{1,0:T(8,128)(2,1)S(1)}, u32[]{:S(2)}, u32[]{:S(2)}) collective-permute-start(bf16[640,384]{1,0:T(8,128)(2,1)S(1)} %collective-permute-done), channel_id=1, source_target_pairs={{0,1},{1,2},{2,3},{3,0},{4,5},{5,6},{6,7},{7,4},{8,9},{9,10},{10,1... | collective-permute-start | bytes 1474568 | tf_op jit(solution)/shard_map/ppermute | solution.py:12
  28.7 12.4 %collective-permute-start.2 = (bf16[640,384]{1,0:T(8,128)(2,1)S(1)}, bf16[640,384]{1,0:T(8,128)(2,1)S(1)}, u32[]{:S(2)}, u32[]{:S(2)}) collective-permute-start(bf16[640,384]{1,0:T(8,128)(2,1)S(1)} %collective-permute-done.1), channel_id=1, source_target_pairs={{0,1},{1,2},{2,3},{3,0},{4,5},{5,6},{6,7},{7,4},{8,9},{9,10},{10,1... | collective-permute-start | bytes 1474568 | tf_op jit(solution)/shard_map/ppermute | solution.py:12
  44.2 28.0 %collective-permute-start.3 = (bf16[640,1536]{1,0:T(8,128)(2,1)S(1)}, bf16[640,1536]{1,0:T(8,128)(2,1)S(1)}, u32[]{:S(2)}, u32[]{:S(2)}) collective-permute-start(bf16[640,1536]{1,0:T(8,128)(2,1)S(1)} %constant_dynamic-slice_fusion), channel_id=1, source_target_pairs={{4,0},{8,4},{12,8},{5,1},{9,5},{13,9},{6,2},{10,6},{14,10},{7,3},{... | collective-permute-start | bytes 5898248 | tf_op jit(solution)/shard_map/ppermute | solution.py:23
